TPU v7x, 32 devices: a whole 2x2x4 slice. The times are simulated.
32 devices in a mesh: ctx: 8 (over z, y), tp: 4 (over x, core).
Axes of the slice: x: 2, y: 2, z: 4, core: 2. Of those that a mesh axis runs over, the one named last changes fastest.
Arguments:
- tokens: bfloat16 [1024, 4096], P('ctx'), may hold values from -6 to 6
- w_query: bfloat16 [4096, 2048], P('ctx', 'tp'), may hold values from -0.09375 to 0.09375
- w_key: bfloat16 [4096, 2048], P('ctx', 'tp'), may hold values from -0.09375 to 0.09375
- w_value: bfloat16 [4096, 2048], P('ctx', 'tp'), may hold values from -0.09375 to 0.09375
- taps_query: float32 [3, 2048], P(None, 'tp'), may hold values from -3.5 to 3.5
- taps_key: float32 [3, 2048], P(None, 'tp'), may hold values from -3.5 to 3.5
- taps_value: float32 [3, 2048], P(None, 'tp'), may hold values from -3.5 to 3.5
- decay_rate: float32 [16, 2048], P(None, 'tp'), may hold values from 1e-05 to 0.03
- residue: float32 [16, 2048], P(None, 'tp'), may hold values from -1.5 to 1.5
- skip_gain: float32 [2048], P('tp'), may hold values from -3 to 3
- w_out: bfloat16 [2048, 4096], P('ctx', 'tp'), may hold values from -0.125 to 0.125
Outputs:
- layer_out: bfloat16 [1024, 4096], P('ctx', 'tp')
All inputs are finite; a program needn't handle non-finite values.
Results may differ from a plain program's by a relative error of at most 0.015.
Values may be sent and summed in bfloat16 or wider, within the bound.
No kernel may reach another device: no remote copies, remote signals or barrier semaphores. Data moves between devices by JAX's collectives and lax.ppermute only.
A program may use at most 128 MiB of HBM per device.

v0:
```python
import jax
import jax.numpy as jnp
from jax import lax
from jax.sharding import PartitionSpec as P


def short_conv(padded, taps):
    return taps[0] * padded[2:] + taps[1] * padded[1:-1] + taps[2] * padded[:-2]


def modal_long_conv(signal, rates, residues, skips):
    length, width = signal.shape
    order = rates.shape[0]
    ctx_count = lax.axis_size("ctx")
    me = lax.axis_index("ctx")
    coefs = residues * jnp.sqrt(2.0 * rates)
    times = jnp.arange(length, dtype=jnp.float32)[:, None, None]
    grow = jnp.exp(rates[None] * times)
    decay = jnp.exp(-rates[None] * times)
    lifted = (grow * signal[:, None, :]).reshape(length, order * width)
    rows = jnp.arange(length, dtype=jnp.int32)
    lower = (rows[:, None] >= rows[None, :]).astype(jnp.float32)
    running = jnp.matmul(lower, lifted, precision=lax.Precision.HIGHEST).reshape(
        length, order, width
    )
    end_state = running[length - 1] * jnp.exp(-rates * (length - 1))
    states = lax.all_gather(end_state, "ctx", axis=0, tiled=False)
    chunk_ids = jnp.arange(ctx_count, dtype=jnp.int32)
    gap = jnp.maximum(me - 1 - chunk_ids, 0).astype(jnp.float32)
    carry_w = jnp.where(
        (chunk_ids < me)[:, None, None], jnp.exp(-rates[None] * (gap[:, None, None] * length)), 0.0
    )
    carried = jnp.sum(carry_w * states, axis=0) * jnp.exp(-rates)
    total = running + carried[None]
    mixed = jnp.sum(coefs[None] * decay * total, axis=1)
    return mixed + skips * signal


def body(
    tokens,
    w_query,
    w_key,
    w_value,
    taps_query,
    taps_key,
    taps_value,
    decay_rate,
    residue,
    skip_gain,
    w_out,
):
    ctx_count = lax.axis_size("ctx")
    halo = lax.ppermute(tokens[-2:], "ctx", perm=[(i, i + 1) for i in range(ctx_count - 1)])
    rows = jnp.concatenate([halo, tokens], axis=0)

    def project(piece):
        full = lax.all_gather(piece, "ctx", axis=0, tiled=True)
        out = jnp.dot(rows, full, preferred_element_type=jnp.float32)
        return out.astype(jnp.bfloat16).astype(jnp.float32)

    queries = project(w_query)
    keys_proj = project(w_key)
    values_proj = project(w_value)
    gate = short_conv(queries, taps_query).astype(jnp.bfloat16)
    product = (short_conv(keys_proj, taps_key) * short_conv(values_proj, taps_value)).astype(
        jnp.bfloat16
    )
    mixed = modal_long_conv(product.astype(jnp.float32), decay_rate, residue, skip_gain)
    mixed = mixed.astype(jnp.bfloat16)
    gated = (gate.astype(jnp.float32) * mixed.astype(jnp.float32)).astype(jnp.bfloat16)
    features = lax.all_gather(gated, "tp", axis=1, tiled=True)
    result = jnp.dot(
        features,
        lax.all_gather(w_out, "ctx", axis=0, tiled=True),
        preferred_element_type=jnp.float32,
    )
    return result.astype(jnp.bfloat16)


def solution(mesh):
    in_specs = (
        P("ctx", None),
        P("ctx", "tp"),
        P("ctx", "tp"),
        P("ctx", "tp"),
        P(None, "tp"),
        P(None, "tp"),
        P(None, "tp"),
        P(None, "tp"),
        P(None, "tp"),
        P("tp"),
        P("ctx", "tp"),
    )
    out_specs = P("ctx", "tp")
    return jax.shard_map(body, mesh=mesh, in_specs=in_specs, out_specs=out_specs, check_vma=False)
```

profile of v0, /device:TPU:0, one launch (start us, length us, event | category | flops | bytes accessed | tf_op | source)
XLA Modules:
  0.0 319.4 jit_solution(1594210370774384721)
XLA Ops:
  6.5 0.0 copy-start.4
  6.5 0.0 all-gather.10.cloned.1.call-start
  6.5 0.7 all-gather.10.cloned.1.call-update
  7.3 0.0 all-gather.8.cloned.1.call-start
  7.3 0.7 all-gather.8.cloned.1.call-update
  8.0 0.0 all-gather.6.cloned.1.call-start
  8.1 0.7 all-gather.6.cloned.1.call-update
  8.7 0.0 all-gather.12.cloned.1.call-start
  8.8 0.5 all-gather.12.cloned.1.call-update
  9.3 0.9 slice.62
  10.2 4.9 %collective-permute-start = (bf16[2,4096]{1,0:T(2,128)(2,1)S(1)}, bf16[2,4096]{1,0:T(2,128)(2,1)S(1)}, u32[]{:S(2)}, u32[]{:S(2)}) collective-permute-start(bf16[2,4096]{1,0:T(2,128)(2,1)S(1)} %slice.62), channel_id=1, source_target_pairs={{0,4},{4,8},{8,12},{12,16},{16,20},{20,24},{24,28},{1,5},{5,9},{9,... | collective-permute-start | bytes 49160 | tf_op jit(solution)/shard_map/ppermute | solution.py:53
  15.1 0.8 fusion.26
  15.9 0.8 fusion.25
  16.7 0.8 fusion.24
  17.5 0.8 copy.12
  18.3 0.0 collective-permute-done
  18.3 67.3 %all-gather.10.cloned.1.call-done = bf16[4096,512]{1,0:T(8,128)(2,1)} async-done(((bf16[512,512]{1,0:T(8,128)(2,1)}), bf16[4096,512]{1,0:T(8,128)(2,1)}) %all-gather.10.cloned.1.call-update) | async-done | bytes 4194320 | tf_op jit(solution)/shard_map/all_gather | solution.py:57
  85.6 3.3 %fusion.8 = f32[130,512]{1,0:T(8,128)S(1)} fusion(bf16[4096,512]{1,0:T(8,128)(2,1)} %all-gather.10.cloned.1.call-done, bf16[128,4096]{1,0:T(8,128)(2,1)} %param.11, bf16[2,4096]{1,0:T(2,128)(2,1)S(1)} %collective-permute-done), kind=kOutput, calls=%fused_computation.11 | convolution fusion | flops 547522560 | bytes 5525504 | tf_op jit(solution)/shard_map/dot_general | solution.py:58
  88.9 70.5 %all-gather.8.cloned.1.call-done = bf16[4096,512]{1,0:T(8,128)(2,1)} async-done(((bf16[512,512]{1,0:T(8,128)(2,1)}), bf16[4096,512]{1,0:T(8,128)(2,1)}) %all-gather.8.cloned.1.call-update) | async-done | bytes 4194320 | tf_op jit(solution)/shard_map/all_gather | solution.py:57
  159.4 0.0 copy-done.4
  159.4 2.9 fusion.9
  162.4 0.2 fusion.20
  162.6 0.5 mul.240
  163.1 3.4 %copy.13 = f32[16,8,16,512]{3,1,2,0:T(8,128)S(1)} copy(f32[16,8,16,512]{3,2,1,0:T(8,128)S(1)} %bitcast.28) | data formatting | bytes 8388608
  166.5 2.9 fusion.2
  169.4 0.0 copy-start.1
  169.5 0.0 copy-start.2
  169.5 5.2 %copy.14 = f32[16,8,16,512]{3,2,1,0:T(8,128)} copy(f32[16,8,16,512]{3,1,2,0:T(8,128)S(1)} %bitcast.26) | data formatting | bytes 8388608
  174.7 0.1 slice_reduce_fusion
  174.8 0.0 copy-done.1
  174.8 0.0 copy-done.2
  174.9 31.8 %all-gather = f32[128,512]{1,0:T(8,128)S(1)} all-gather(f32[16,512]{1,0:T(8,128)S(1)} %get-tuple-element.6), channel_id=2, replica_groups=mesh['ctx'=8,'tp'=4] {'ctx'}, dimensions={0}, use_global_device_ids=true | all-gather | bytes 294912 | tf_op jit(solution)/shard_map/all_gather | solution.py:27
  206.7 0.1 multiply_reduce_fusion
  206.8 0.0 copy-start.3
  206.8 28.2 %all-gather.6.cloned.1.call-done = bf16[4096,512]{1,0:T(8,128)(2,1)} async-done(((bf16[512,512]{1,0:T(8,128)(2,1)}), bf16[4096,512]{1,0:T(8,128)(2,1)}) %all-gather.6.cloned.1.call-update) | async-done | bytes 4194320 | tf_op jit(solution)/shard_map/all_gather | solution.py:57
  235.0 0.0 copy-start
  235.0 3.1 fusion.10
  238.1 0.3 copy-done
  238.4 1.5 fusion.1
  239.9 0.0 copy-done.3
  239.9 0.1 multiply_convert_fusion
  240.1 7.2 %all_gather.26 = bf16[128,2048]{1,0:T(8,128)(2,1)S(1)} all-gather(bf16[128,512]{1,0:T(8,128)(2,1)S(1)} %multiply_convert_fusion), channel_id=1, replica_groups=mesh['ctx'=8,'tp'=4] {'tp'}, dimensions={1}, use_global_device_ids=true | all-gather | bytes 655360 | tf_op jit(solution)/shard_map/all_gather | solution.py:71
  247.2 62.0 %all-gather.12.cloned.1.call-done = bf16[2048,1024]{1,0:T(8,128)(2,1)} async-done(((bf16[256,1024]{1,0:T(8,128)(2,1)}), bf16[2048,1024]{1,0:T(8,128)(2,1)}) %all-gather.12.cloned.1.call-update) | async-done | bytes 4194320 | tf_op jit(solution)/shard_map/all_gather | solution.py:74
  309.2 3.6 %convolution_convert_fusion = bf16[128,1024]{1,0:T(8,128)(2,1)} fusion(bf16[128,2048]{1,0:T(8,128)(2,1)S(1)} %all_gather.26, bf16[2048,1024]{1,0:T(8,128)(2,1)} %all-gather.12.cloned.1.call-done), kind=kOutput, calls=%fused_computation.9 | convolution fusion | flops 537001984 | bytes 4980736 | tf_op jit(solution)/shard_map/dot_general | solution.py:72
  (5 shorter events, 0.1 us)
Async XLA Ops:
  6.5 152.9 %copy-start.4 = (bf16[128,4096]{1,0:T(8,128)(2,1)S(1)}, bf16[128,4096]{1,0:T(8,128)(2,1)}, u32[]{:S(2)}) copy-start(bf16[128,4096]{1,0:T(8,128)(2,1)} %param.11) | copy-start | bytes 3145732
  6.5 79.1 %all-gather.10.cloned.1.call-start = ((), (), s32[]{:S(2)}) async-start(), calls=%async_computation.2 | async-start | bytes 4718592 | tf_op jit(solution)/shard_map/all_gather | solution.py:57
  7.3 152.2 %all-gather.8.cloned.1.call-start = ((), (), s32[]{:S(2)}) async-start(), calls=%async_computation.1 | async-start | bytes 4718592 | tf_op jit(solution)/shard_map/all_gather | solution.py:57
  8.0 227.0 %all-gather.6.cloned.1.call-start = ((), (), s32[]{:S(2)}) async-start(), calls=%async_computation | async-start | bytes 4718592 | tf_op jit(solution)/shard_map/all_gather | solution.py:57
  8.7 300.5 %all-gather.12.cloned.1.call-start = ((), (), s32[]{:S(2)}) async-start(), calls=%async_computation.3 | async-start | bytes 4718592 | tf_op jit(solution)/shard_map/all_gather | solution.py:74
  10.2 8.1 %collective-permute-start = (bf16[2,4096]{1,0:T(2,128)(2,1)S(1)}, bf16[2,4096]{1,0:T(2,128)(2,1)S(1)}, u32[]{:S(2)}, u32[]{:S(2)}) collective-permute-start(bf16[2,4096]{1,0:T(2,128)(2,1)S(1)} %slice.62), channel_id=1, source_target_pairs={{0,4},{4,8},{8,12},{12,16},{16,20},{20,24},{24,28},{1,5},{5,9},{9,... | collective-permute-start | bytes 49160 | tf_op jit(solution)/shard_map/ppermute | solution.py:53
  169.4 5.4 %copy-start.1 = (f32[16,512]{1,0:T(8,128)S(1)}, f32[16,512]{1,0:T(8,128)}, u32[]{:S(2)}) copy-start(f32[16,512]{1,0:T(8,128)} %param.18) | copy-start | bytes 98308
  169.5 5.4 %copy-start.2 = (f32[16,512]{1,0:T(8,128)S(1)}, f32[16,512]{1,0:T(8,128)}, u32[]{:S(2)}) copy-start(f32[16,512]{1,0:T(8,128)} %param.19) | copy-start | bytes 98308
  206.8 33.1 %copy-start.3 = (f32[512]{0:T(512)S(1)}, f32[512]{0:T(512)}, u32[]{:S(2)}) copy-start(f32[512]{0:T(512)} %param.20) | copy-start | bytes 6148
  235.0 3.4 %copy-start = (f32[16,8,16,512]{3,2,1,0:T(8,128)S(1)}, f32[16,8,16,512]{3,2,1,0:T(8,128)}, u32[]{:S(2)}) copy-start(f32[16,8,16,512]{3,2,1,0:T(8,128)} %copy.14) | copy-start | bytes 12582916
Sparse Core Ops, SparseCore 0:
  9.5 76.0 all-gather.9
  87.7 71.6 all-gather.7
  161.6 73.3 all-gather.5
  237.0 72.2 all-gather.11
where the time goes:
time: 320 us; the launch traced here: 319 us
  waiting for transfers between devices  231 us (72%)
  blocking collectives  39 us (12%)
  matrix products  15.8 us (5%)
  local copies, waits for them, and re-layouts  13.7 us (4%)
  between operations  13.3 us (4%)
  starting transfers between devices  4.99 us (2%)
    all_gather x3, waiting for transfers between devices, project(): full = lax.all_gather(piece, 'ctx', axis=0, tiled=True)  166 us
    all_gather x1, waiting for transfers between devices, body(): lax.all_gather(w_out, 'ctx', axis=0, tiled=True)  62 us
    all_gather x1, blocking collectives, modal_long_conv(): states = lax.all_gather(end_state, 'ctx', axis=0, tiled=False)  31.8 us
    unnamed x13, local copies, waits for them, and re-layouts  9.79 us
    dot_general x3, matrix products, project(): out = jnp.dot(rows, full, preferred_element_type=jnp.float32)  9.3 us
    all_gather x1, blocking collectives, body(): features = lax.all_gather(gated, 'tp', axis=1, tiled=True)  7.19 us
  transfers between devices with their start and end apart: 5, of which 4 were waited for; matrix products, arithmetic and copies ran while one was open for 9% of the time, Pallas kernels for 0%

commit v1 on v0

--- a/solution.py
+++ b/solution.py
@@ -2,6 +2,19 @@
 import jax.numpy as jnp
 from jax import lax
 from jax.sharding import PartitionSpec as P
+
+
+def collect(array, axis, dim):
+    ways = lax.axis_size(axis)
+    up = [(d, (d + 1) % ways) for d in range(ways)]
+    down = [(d, (d - 1) % ways) for d in range(ways)]
+    earlier, later = ([array], [array])
+    for _ in range(ways // 2):
+        earlier.append(lax.ppermute(earlier[-1], axis, up))
+    for _ in range((ways - 1) // 2):
+        later.append(lax.ppermute(later[-1], axis, down))
+    line = jnp.concatenate([*earlier[::-1], *later[1:]], axis=dim)
+    return jnp.roll(line, (lax.axis_index(axis) - ways // 2) * array.shape[dim], axis=dim)
 
 
 def short_conv(padded, taps):
@@ -69,11 +82,7 @@
     mixed = mixed.astype(jnp.bfloat16)
     gated = (gate.astype(jnp.float32) * mixed.astype(jnp.float32)).astype(jnp.bfloat16)
     features = lax.all_gather(gated, "tp", axis=1, tiled=True)
-    result = jnp.dot(
-        features,
-        lax.all_gather(w_out, "ctx", axis=0, tiled=True),
-        preferred_element_type=jnp.float32,
-    )
+    result = jnp.dot(features, collect(w_out, "ctx", 0), preferred_element_type=jnp.float32)
     return result.astype(jnp.bfloat16)
 
 

time: 320 us -> 308 us (0.963)
  waiting for transfers between devices: 231 us -> 190 us
  local copies, waits for them, and re-layouts: 13.7 us -> 29.2 us
  starting transfers between devices: 4.99 us -> 18.3 us
    ppermute x0 -> x7, waiting for transfers between devices: none -> 89.9 us  [the longest x4 78.3 us: collect(): earlier.append(lax.ppermute(earlier[-1], axis, up))]
    all_gather x3, waiting for transfers between devices: 166 us -> 98 us  [project(): full = lax.all_gather(piece, 'ctx', axis=0, tiled=True)]
    all_gather x1 -> x0, waiting for transfers between devices: 62 us -> none  [body(): lax.all_gather(w_out, 'ctx', axis=0, tiled=True)]
    ppermute x0 -> x7, starting transfers between devices: none -> 15.1 us  [the longest x3 9.23 us: collect(): later.append(lax.ppermute(later[-1], axis, down))]
    unnamed x13 -> x30, local copies, waits for them, and re-layouts: 9.79 us -> 24.4 us
  transfers between devices with their start and end apart: 5 -> 11, of which waited for: 4 -> 8; matrix products, arithmetic and copies ran while one was open for 9% -> 12% of each run, Pallas kernels for 0% -> 0%
where the time goes in v1:
time: 308 us
  waiting for transfers between devices  190 us (62%)
  blocking collectives  38.9 us (13%)
  local copies, waits for them, and re-layouts  29.2 us (9%)
  starting transfers between devices  18.3 us (6%)
  matrix products  15.8 us (5%)
  between operations  13.3 us (4%)
    all_gather x3, waiting for transfers between devices, project(): full = lax.all_gather(piece, 'ctx', axis=0, tiled=True)  98 us
    ppermute x4, waiting for transfers between devices, collect(): earlier.append(lax.ppermute(earlier[-1], axis, up))  78.3 us
    all_gather x1, blocking collectives, modal_long_conv(): states = lax.all_gather(end_state, 'ctx', axis=0, tiled=False)  31.8 us
    unnamed x30, local copies, waits for them, and re-layouts  24.4 us
    ppermute x3, waiting for transfers between devices, collect(): later.append(lax.ppermute(later[-1], axis, down))  11.6 us
    dot_general x3, matrix products, project(): out = jnp.dot(rows, full, preferred_element_type=jnp.float32)  9.24 us
    ppermute x3, starting transfers between devices, collect(): later.append(lax.ppermute(later[-1], axis, down))  9.23 us
    all_gather x1, blocking collectives, body(): features = lax.all_gather(gated, 'tp', axis=1, tiled=True)  7.15 us
  transfers between devices with their start and end apart: 11, of which 8 were waited for; matrix products, arithmetic and copies ran while one was open for 12% of the time, Pallas kernels for 0%

profile of v1, /device:TPU:0, one launch (start us, length us, event | category | flops | bytes accessed | tf_op | source)
XLA Modules:
  0.0 307.5 jit_solution(10907013143696413552)
XLA Ops:
  6.5 0.7 all-gather.7.cloned.1.call-update
  7.3 0.0 all-gather.9.cloned.1.call-start
  7.3 0.7 all-gather.9.cloned.1.call-update
  8.0 0.0 all-gather.5.cloned.1.call-start
  8.1 0.7 all-gather.5.cloned.1.call-update
  8.7 3.0 collective-permute-start.1
  11.8 16.8 %collective-permute-done.1 = bf16[256,1024]{1,0:T(8,128)(2,1)S(1)} collective-permute-done((bf16[256,1024]{1,0:T(8,128)(2,1)}, bf16[256,1024]{1,0:T(8,128)(2,1)S(1)}, u32[]{:S(2)}, u32[]{:S(2)}) %collective-permute-start.1) | collective-permute-done | bytes 524320 | tf_op jit(solution)/shard_map/ppermute | solution.py:13
  28.6 0.4 collective-permute-start.2
  29.0 4.4 %collective-permute-start.5 = (bf16[256,1024]{1,0:T(8,128)(2,1)}, bf16[256,1024]{1,0:T(8,128)(2,1)S(1)}, u32[]{:S(2)}, u32[]{:S(2)}) collective-permute-start(bf16[256,1024]{1,0:T(8,128)(2,1)} %param.21), channel_id=1, source_target_pairs={{0,28},{4,0},{8,4},{12,8},{16,12},{20,16},{24,20},{28,24},{1,29},{... | collective-permute-start | bytes 1572872 | tf_op jit(solution)/shard_map/ppermute | solution.py:15
  33.3 21.8 %collective-permute-done.2 = bf16[256,1024]{1,0:T(8,128)(2,1)S(1)} collective-permute-done((bf16[256,1024]{1,0:T(8,128)(2,1)S(1)}, bf16[256,1024]{1,0:T(8,128)(2,1)S(1)}, u32[]{:S(2)}, u32[]{:S(2)}) %collective-permute-start.2) | collective-permute-done | bytes 524320 | tf_op jit(solution)/shard_map/ppermute | solution.py:13
  55.1 0.0 collective-permute-start.3
  55.1 0.9 slice.62
  56.0 3.2 %collective-permute-start = (bf16[2,4096]{1,0:T(2,128)(2,1)S(1)}, bf16[2,4096]{1,0:T(2,128)(2,1)S(1)}, u32[]{:S(2)}, u32[]{:S(2)}) collective-permute-start(bf16[2,4096]{1,0:T(2,128)(2,1)S(1)} %slice.62), channel_id=1, source_target_pairs={{0,4},{4,8},{8,12},{12,16},{16,20},{20,24},{24,28},{1,5},{5,9},{9,... | collective-permute-start | bytes 49160 | tf_op jit(solution)/shard_map/ppermute | solution.py:66
  59.2 0.8 copy.12
  60.0 0.8 fusion.30
  60.8 0.0 collective-permute-done.5
  60.8 2.9 collective-permute-start.6
  63.7 24.5 %collective-permute-done.3 = bf16[256,1024]{1,0:T(8,128)(2,1)S(1)} collective-permute-done((bf16[256,1024]{1,0:T(8,128)(2,1)S(1)}, bf16[256,1024]{1,0:T(8,128)(2,1)S(1)}, u32[]{:S(2)}, u32[]{:S(2)}) %collective-permute-start.3) | collective-permute-done | bytes 524320 | tf_op jit(solution)/shard_map/ppermute | solution.py:13
  88.2 2.5 collective-permute-start.4
  90.7 0.8 fusion.31
  91.5 0.8 fusion.32
  92.3 11.6 %collective-permute-done.6 = bf16[256,1024]{1,0:T(8,128)(2,1)S(1)} collective-permute-done((bf16[256,1024]{1,0:T(8,128)(2,1)S(1)}, bf16[256,1024]{1,0:T(8,128)(2,1)S(1)}, u32[]{:S(2)}, u32[]{:S(2)}) %collective-permute-start.6) | collective-permute-done | bytes 524320 | tf_op jit(solution)/shard_map/ppermute | solution.py:15
  103.9 2.0 collective-permute-start.7
  105.9 15.2 %collective-permute-done.4 = bf16[256,1024]{1,0:T(8,128)(2,1)S(1)} collective-permute-done((bf16[256,1024]{1,0:T(8,128)(2,1)S(1)}, bf16[256,1024]{1,0:T(8,128)(2,1)S(1)}, u32[]{:S(2)}, u32[]{:S(2)}) %collective-permute-start.4) | collective-permute-done | bytes 524320 | tf_op jit(solution)/shard_map/ppermute | solution.py:13
  121.1 0.8 constant_dynamic-update-slice_fusion.15
  121.9 0.8 constant_dynamic-update-slice_fusion.14
  122.8 0.9 constant_dynamic-update-slice_fusion.13
  123.6 0.8 constant_dynamic-update-slice_fusion.12
  124.5 0.8 constant_dynamic-update-slice_fusion.11
  125.3 0.8 constant_dynamic-update-slice_fusion.10
  126.2 0.8 constant_dynamic-update-slice_fusion.9
  127.0 0.0 collective-permute-done.7
  127.0 0.8 constant_dynamic-update-slice_fusion.8
  127.8 0.8 constant_dynamic-update-slice_fusion.7
  128.7 0.8 constant_dynamic-update-slice_fusion.6
  129.5 0.9 constant_dynamic-update-slice_fusion.5
  130.4 0.8 constant_dynamic-update-slice_fusion.4
  131.2 0.8 constant_dynamic-update-slice_fusion.3
  132.0 0.8 constant_dynamic-update-slice_fusion.2
  132.9 0.8 constant_dynamic-update-slice_fusion.1
  133.7 0.9 constant_dynamic-update-slice_fusion
  134.6 0.0 collective-permute-done
  134.6 1.6 all-gather.7.cloned.1.call-done
  136.2 3.3 %fusion.14 = f32[130,512]{1,0:T(8,128)S(1)} fusion(bf16[4096,512]{1,0:T(8,128)(2,1)} %all-gather.7.cloned.1.call-done, bf16[128,4096]{1,0:T(8,128)(2,1)} %param.11, bf16[2,4096]{1,0:T(2,128)(2,1)S(1)} %collective-permute-done), kind=kOutput, calls=%fused_computation.15 | convolution fusion | flops 547522560 | bytes 5525504 | tf_op jit(solution)/shard_map/dot_general | solution.py:71
  139.5 72.1 %all-gather.9.cloned.1.call-done = bf16[4096,512]{1,0:T(8,128)(2,1)} async-done(((bf16[512,512]{1,0:T(8,128)(2,1)}), bf16[4096,512]{1,0:T(8,128)(2,1)}) %all-gather.9.cloned.1.call-update) | async-done | bytes 4194320 | tf_op jit(solution)/shard_map/all_gather | solution.py:70
  211.6 3.0 fusion.13
  214.6 0.2 fusion.25
  214.8 0.5 mul.243
  215.3 3.4 %copy.13 = f32[16,8,16,512]{3,1,2,0:T(8,128)S(1)} copy(f32[16,8,16,512]{3,2,1,0:T(8,128)S(1)} %bitcast.27) | data formatting | bytes 8388608
  218.8 2.9 fusion.4
  221.7 1.9 copy-done
  223.6 0.1 slice_reduce_fusion
  223.7 0.0 copy-start.2
  223.7 0.0 copy-start.3
  223.8 5.6 %copy.14 = f32[16,8,16,512]{3,2,1,0:T(8,128)S(1)} copy(f32[16,8,16,512]{3,1,2,0:T(8,128)} %bitcast.25) | data formatting | bytes 8388608
  229.4 31.8 %all-gather = f32[128,512]{1,0:T(8,128)S(1)} all-gather(f32[16,512]{1,0:T(8,128)S(1)} %get-tuple-element.6), channel_id=2, replica_groups=mesh['ctx'=8,'tp'=4] {'ctx'}, dimensions={0}, use_global_device_ids=true | all-gather | bytes 294912 | tf_op jit(solution)/shard_map/all_gather | solution.py:40
  261.2 0.1 multiply_reduce_fusion
  261.4 0.0 copy-start.4
  261.4 1.5 fusion.1
  262.8 24.2 %all-gather.5.cloned.1.call-done = bf16[4096,512]{1,0:T(8,128)(2,1)} async-done(((bf16[512,512]{1,0:T(8,128)(2,1)}), bf16[4096,512]{1,0:T(8,128)(2,1)}) %all-gather.5.cloned.1.call-update) | async-done | bytes 4194320 | tf_op jit(solution)/shard_map/all_gather | solution.py:70
  287.1 3.0 fusion.15
  290.1 0.1 multiply_convert_fusion
  290.2 7.1 %all_gather.23 = bf16[128,2048]{1,0:T(8,128)(2,1)S(1)} all-gather(bf16[128,512]{1,0:T(8,128)(2,1)S(1)} %multiply_convert_fusion), channel_id=1, replica_groups=mesh['ctx'=8,'tp'=4] {'tp'}, dimensions={1}, use_global_device_ids=true | all-gather | bytes 655360 | tf_op jit(solution)/shard_map/all_gather | solution.py:84
  297.4 3.6 %fusion.10 = bf16[128,1024]{1,0:T(8,128)(2,1)} fusion(bf16[128,2048]{1,0:T(8,128)(2,1)S(1)} %all_gather.23, bf16[4096,1024]{1,0:T(8,128)(2,1)} %constant_dynamic-update-slice_fusion, s32[]{:T(128)S(6)} %select_n.19), kind=kOutput, calls=%fused_computation.11 | convolution fusion | flops 537001984 | bytes 4980740 | tf_op jit(solution)/shard_map/dot_general | solution.py:85
  (14 shorter events, 0.1 us)
Async XLA Ops:
  6.5 117.9 %copy-start.1 = (bf16[256,1024]{1,0:T(8,128)(2,1)S(1)}, bf16[256,1024]{1,0:T(8,128)(2,1)}, u32[]{:S(2)}) copy-start(bf16[256,1024]{1,0:T(8,128)(2,1)} %param.21) | copy-start | bytes 1572868
  6.5 129.7 %all-gather.7.cloned.1.call-start = ((), (), s32[]{:S(2)}) async-start(), calls=%async_computation.1 | async-start | bytes 4718592 | tf_op jit(solution)/shard_map/all_gather | solution.py:70
  7.3 204.4 %all-gather.9.cloned.1.call-start = ((), (), s32[]{:S(2)}) async-start(), calls=%async_computation.2 | async-start | bytes 4718592 | tf_op jit(solution)/shard_map/all_gather | solution.py:70
  8.0 279.1 %all-gather.5.cloned.1.call-start = ((), (), s32[]{:S(2)}) async-start(), calls=%async_computation | async-start | bytes 4718592 | tf_op jit(solution)/shard_map/all_gather | solution.py:70
  8.7 19.9 %collective-permute-start.1 = (bf16[256,1024]{1,0:T(8,128)(2,1)}, bf16[256,1024]{1,0:T(8,128)(2,1)S(1)}, u32[]{:S(2)}, u32[]{:S(2)}) collective-permute-start(bf16[256,1024]{1,0:T(8,128)(2,1)} %param.21), channel_id=1, source_target_pairs={{0,4},{4,8},{8,12},{12,16},{16,20},{20,24},{24,28},{28,0},{1,5},{5... | collective-permute-start | bytes 1572872 | tf_op jit(solution)/shard_map/ppermute | solution.py:13
  28.6 26.5 %collective-permute-start.2 = (bf16[256,1024]{1,0:T(8,128)(2,1)S(1)}, bf16[256,1024]{1,0:T(8,128)(2,1)S(1)}, u32[]{:S(2)}, u32[]{:S(2)}) collective-permute-start(bf16[256,1024]{1,0:T(8,128)(2,1)S(1)} %collective-permute-done.1), channel_id=1, source_target_pairs={{0,4},{4,8},{8,12},{12,16},{16,20},{20,24},{24,28},{28,0},{1,5},{5... | collective-permute-start | bytes 1572872 | tf_op jit(solution)/shard_map/ppermute | solution.py:13
  29.0 31.8 %collective-permute-start.5 = (bf16[256,1024]{1,0:T(8,128)(2,1)}, bf16[256,1024]{1,0:T(8,128)(2,1)S(1)}, u32[]{:S(2)}, u32[]{:S(2)}) collective-permute-start(bf16[256,1024]{1,0:T(8,128)(2,1)} %param.21), channel_id=1, source_target_pairs={{0,28},{4,0},{8,4},{12,8},{16,12},{20,16},{24,20},{28,24},{1,29},{... | collective-permute-start | bytes 1572872 | tf_op jit(solution)/shard_map/ppermute | solution.py:15
  55.1 33.1 %collective-permute-start.3 = (bf16[256,1024]{1,0:T(8,128)(2,1)S(1)}, bf16[256,1024]{1,0:T(8,128)(2,1)S(1)}, u32[]{:S(2)}, u32[]{:S(2)}) collective-permute-start(bf16[256,1024]{1,0:T(8,128)(2,1)S(1)} %collective-permute-done.2), channel_id=1, source_target_pairs={{0,4},{4,8},{8,12},{12,16},{16,20},{20,24},{24,28},{28,0},{1,5},{5... | collective-permute-start | bytes 1572872 | tf_op jit(solution)/shard_map/ppermute | solution.py:13
  56.0 78.6 %collective-permute-start = (bf16[2,4096]{1,0:T(2,128)(2,1)S(1)}, bf16[2,4096]{1,0:T(2,128)(2,1)S(1)}, u32[]{:S(2)}, u32[]{:S(2)}) collective-permute-start(bf16[2,4096]{1,0:T(2,128)(2,1)S(1)} %slice.62), channel_id=1, source_target_pairs={{0,4},{4,8},{8,12},{12,16},{16,20},{20,24},{24,28},{1,5},{5,9},{9,... | collective-permute-start | bytes 49160 | tf_op jit(solution)/shard_map/ppermute | solution.py:66
  60.8 43.1 %collective-permute-start.6 = (bf16[256,1024]{1,0:T(8,128)(2,1)S(1)}, bf16[256,1024]{1,0:T(8,128)(2,1)S(1)}, u32[]{:S(2)}, u32[]{:S(2)}) collective-permute-start(bf16[256,1024]{1,0:T(8,128)(2,1)S(1)} %collective-permute-done.5), channel_id=1, source_target_pairs={{0,28},{4,0},{8,4},{12,8},{16,12},{20,16},{24,20},{28,24},{1,29},{... | collective-permute-start | bytes 1572872 | tf_op jit(solution)/shard_map/ppermute | solution.py:15
  88.2 32.9 %collective-permute-start.4 = (bf16[256,1024]{1,0:T(8,128)(2,1)S(1)}, bf16[256,1024]{1,0:T(8,128)(2,1)S(1)}, u32[]{:S(2)}, u32[]{:S(2)}) collective-permute-start(bf16[256,1024]{1,0:T(8,128)(2,1)S(1)} %collective-permute-done.3), channel_id=1, source_target_pairs={{0,4},{4,8},{8,12},{12,16},{16,20},{20,24},{24,28},{28,0},{1,5},{5... | collective-permute-start | bytes 1572872 | tf_op jit(solution)/shard_map/ppermute | solution.py:13
  103.9 23.1 %collective-permute-start.7 = (bf16[256,1024]{1,0:T(8,128)(2,1)S(1)}, bf16[256,1024]{1,0:T(8,128)(2,1)S(1)}, u32[]{:S(2)}, u32[]{:S(2)}) collective-permute-start(bf16[256,1024]{1,0:T(8,128)(2,1)S(1)} %collective-permute-done.6), channel_id=1, source_target_pairs={{0,28},{4,0},{8,4},{12,8},{16,12},{20,16},{24,20},{28,24},{1,29},{... | collective-permute-start | bytes 1572872 | tf_op jit(solution)/shard_map/ppermute | solution.py:15
  132.9 78.8 %copy-start.5 = (bf16[128,4096]{1,0:T(8,128)(2,1)S(1)}, bf16[128,4096]{1,0:T(8,128)(2,1)}, u32[]{:S(2)}) copy-start(bf16[128,4096]{1,0:T(8,128)(2,1)} %param.11) | copy-start | bytes 3145732
  221.7 1.9 copy-start
  223.7 5.7 %copy-start.2 = (f32[16,512]{1,0:T(8,128)S(1)}, f32[16,512]{1,0:T(8,128)}, u32[]{:S(2)}) copy-start(f32[16,512]{1,0:T(8,128)} %param.18) | copy-start | bytes 98308
  223.7 5.7 %copy-start.3 = (f32[16,512]{1,0:T(8,128)S(1)}, f32[16,512]{1,0:T(8,128)}, u32[]{:S(2)}) copy-start(f32[16,512]{1,0:T(8,128)} %param.19) | copy-start | bytes 98308
  261.4 28.7 %copy-start.4 = (f32[512]{0:T(512)S(1)}, f32[512]{0:T(512)}, u32[]{:S(2)}) copy-start(f32[512]{0:T(512)} %param.20) | copy-start | bytes 6148
Sparse Core Ops, SparseCore 0:
  9.5 126.7 all-gather.6
  138.4 73.2 all-gather.8
  213.8 73.2 all-gather.4
